TPU v7x, 256 devices: a whole 4x4x8 slice. The times are simulated.
256 devices in a mesh: layer: 2 (over core), feat: 4 (over x), tok: 32 (over z, y).
Axes of the slice: x: 4, y: 4, z: 8, core: 2. Of those that a mesh axis runs over, the one named last changes fastest.
Arguments:
- resid_in: bfloat16 [8192, 2304], P('tok', 'feat'), may hold values from -6 to 6
- attn_out: bfloat16 [2, 8192, 2304], P('layer', 'tok', 'feat'), may hold values from -4 to 4
- carry_in: bfloat16 [8192, 2304], P('tok', 'feat'), may hold values from -4 to 4
- enc_weight: bfloat16 [2, 2304, 8192], P('layer', None, 'feat'), may hold values from -0.125 to 0.125
- enc_bias: float32 [2, 8192], P('layer', 'feat'), may hold values from -3 to 3
- dec_own: bfloat16 [2, 8192, 2304], P('layer', 'feat', 'tok'), may hold values from -0.125 to 0.125
- dec_next: bfloat16 [2, 8192, 2304], P('layer', 'feat', 'tok'), may hold values from -0.125 to 0.125
- block_list: int32 [2, 64, 32], P('layer', 'tok'), may hold values from 0 to 63, all different within a row
- block_count: int32 [2, 64], P('layer', 'tok'), may hold values from 8 to 32, as said below
Outputs:
- reconstruction: bfloat16 [2, 8192, 2304], P('layer', 'tok', 'feat')
- outgoing: bfloat16 [2, 8192, 2304], P('layer', 'tok', 'feat')
Inputs may be any that keep to these rules, and one draw needn't show every extreme that they name: Each row of block_list names 32 different blocks; only its first block_count entries are in use. `block_count`: some entry equals 32.
All inputs are finite; a program needn't handle non-finite values.
Results may differ from a plain program's by a relative error of at most 0.015.
Values may be sent and summed in bfloat16 or wider, within the bound.
No kernel may reach another device: no remote copies, remote signals or barrier semaphores. Data moves between devices by JAX's collectives and lax.ppermute only.
A program may use at most 128 MiB of HBM per device.

v0:
```python
import jax
import jax.numpy as jnp
from jax import lax
from jax.sharding import PartitionSpec as P

BLOCK = 128
TILE = 128


def from_behind(shard, axis, by):
    length = lax.axis_size(axis)
    pairs = [(i, i + by) for i in range(length) if 0 <= i + by < length]
    return lax.ppermute(shard, axis, pairs)


def block_mask(block_list, block_count, tile_index, feat_index, blocks_dev):
    listed = lax.dynamic_index_in_dim(block_list[0], tile_index, 0, keepdims=False)
    count_now = lax.dynamic_index_in_dim(block_count[0], tile_index, 0, keepdims=False)
    in_use = jnp.arange(listed.shape[0], dtype=jnp.int32) < count_now
    own_blocks = feat_index * blocks_dev + jnp.arange(blocks_dev, dtype=jnp.int32)
    matches = (listed[None, :] == own_blocks[:, None]) & in_use[None, :]
    return jnp.any(matches, axis=1)


def decode_every(gathered, enc_weight, enc_bias, decoders, active):
    preact = (
        jnp.dot(gathered, enc_weight[0], preferred_element_type=jnp.float32) + enc_bias[0][None, :]
    )
    feat_mask = jnp.repeat(active.astype(jnp.float32), BLOCK)
    features = (jax.nn.relu(preact) * feat_mask[None, :]).astype(jnp.bfloat16)
    own_part = jnp.dot(features, decoders[0], preferred_element_type=jnp.float32)
    next_part = jnp.dot(features, decoders[1], preferred_element_type=jnp.float32)
    return jnp.stack([own_part, next_part])


def store_rows(holder, values, row_start, is_valid):
    previous = lax.dynamic_slice_in_dim(holder, row_start, values.shape[0], 0)
    return lax.dynamic_update_slice_in_dim(
        holder, jnp.where(is_valid, values, previous), row_start, 0
    )


def shards(
    resid_in, attn_out, carry_in, enc_weight, enc_bias, dec_own, dec_next, block_list, block_count
):
    layer_count = lax.axis_size("layer")
    section_index = lax.axis_index("layer")
    feat_index = lax.axis_index("feat")
    tile_count = block_count.shape[1]
    columns = resid_in.shape[1]
    blocks_dev = enc_weight.shape[2] // BLOCK
    decoders = (
        lax.all_gather(dec_own[0], "tok", axis=1, tiled=True),
        lax.all_gather(dec_next[0], "tok", axis=1, tiled=True),
    )
    empty_rows = jnp.zeros((resid_in.shape[0], columns), jnp.bfloat16)
    nothing_yet = jnp.zeros((2, TILE, columns), jnp.bfloat16)

    def advance(step_index, state_tuple):
        arrived, recon_holder, outgoing_holder = state_tuple
        tile_index = step_index - section_index
        is_valid = (tile_index >= 0) & (tile_index < tile_count)
        tile_index = jnp.clip(tile_index, 0, tile_count - 1)
        row_start = tile_index * TILE
        first_section = section_index == 0
        residual = jnp.where(
            first_section, lax.dynamic_slice_in_dim(resid_in, row_start, TILE, 0), arrived[0]
        )
        incoming = jnp.where(
            first_section, lax.dynamic_slice_in_dim(carry_in, row_start, TILE, 0), arrived[1]
        )
        gathered = lax.all_gather(residual, "feat", axis=1, tiled=True)
        active = block_mask(block_list, block_count, tile_index, feat_index, blocks_dev)
        zero_terms = jnp.zeros((2, TILE, gathered.shape[1]), jnp.float32)
        terms = lax.cond(
            is_valid,
            lambda source: decode_every(source, enc_weight, enc_bias, decoders, active),
            lambda source: zero_terms,
            gathered,
        )
        summed = lax.psum_scatter(
            terms.astype(jnp.bfloat16), "feat", scatter_dimension=2, tiled=True
        ).astype(jnp.float32)
        attention = lax.dynamic_slice_in_dim(attn_out[0], row_start, TILE, 0)
        recon_now = summed[0] + incoming.astype(jnp.float32)
        new_residual = (
            residual.astype(jnp.float32) + attention.astype(jnp.float32) + recon_now
        ).astype(jnp.bfloat16)
        outgoing_now = summed[1].astype(jnp.bfloat16)
        recon_holder = store_rows(recon_holder, recon_now.astype(jnp.bfloat16), row_start, is_valid)
        outgoing_holder = store_rows(outgoing_holder, outgoing_now, row_start, is_valid)
        arrived = from_behind(jnp.stack([new_residual, outgoing_now]), "layer", 1)
        return (arrived, recon_holder, outgoing_holder)

    finished = lax.fori_loop(
        0, tile_count + layer_count - 1, advance, (nothing_yet, empty_rows, empty_rows)
    )
    return (finished[1][None], finished[2][None])


def solution(mesh):
    return jax.shard_map(
        shards,
        mesh=mesh,
        in_specs=(
            P("tok", "feat"),
            P("layer", "tok", "feat"),
            P("tok", "feat"),
            P("layer", None, "feat"),
            P("layer", "feat"),
            P("layer", "feat", "tok"),
            P("layer", "feat", "tok"),
            P("layer", "tok", None),
            P("layer", "tok"),
        ),
        out_specs=(P("layer", "tok", "feat"), P("layer", "tok", "feat")),
        check_vma=False,
    )
```

profile of v0, /device:TPU:1, one launch (start us, length us, event | category | flops | bytes accessed | tf_op | source)
XLA Modules:
  0.0 485.6 jit_solution(13964440871166911584)
XLA Ops:
  7.2 0.0 all-gather.5.cloned.1.call-start
  7.2 0.7 all-gather.5.cloned.1.call-update
  7.9 0.0 all-gather.7.cloned.1.call-start
  7.9 0.7 all-gather.7.cloned.1.call-update
  8.7 108.2 %all-gather.5.cloned.1.call-done = bf16[1,2048,2304]{1,2,0:T(8,128)(2,1)} async-done(((bf16[1,2048,72]{1,2,0:T(8,128)(2,1)}), bf16[1,2048,2304]{1,2,0:T(8,128)(2,1)}) %all-gather.5.cloned.1.call-update) | async-done | bytes 9437200 | tf_op jit(solution)/shard_map/all_gather | solution.py:53
  116.8 12.4 %copy.26 = bf16[2048,2304]{1,0:T(8,128)(2,1)} copy(bf16[2048,2304]{0,1:T(8,128)(2,1)} %bitcast.82) | data formatting | bytes 18874368 | tf_op jit(solution)/shard_map/while | solution.py:95
  129.2 90.5 %all-gather.7.cloned.1.call-done = bf16[1,2048,2304]{1,2,0:T(8,128)(2,1)} async-done(((bf16[1,2048,72]{1,2,0:T(8,128)(2,1)}), bf16[1,2048,2304]{1,2,0:T(8,128)(2,1)}) %all-gather.7.cloned.1.call-update) | async-done | bytes 9437200 | tf_op jit(solution)/shard_map/all_gather | solution.py:54
  219.8 12.8 %copy.27 = bf16[2048,2304]{1,0:T(8,128)(2,1)} copy(bf16[2048,2304]{0,1:T(8,128)(2,1)} %bitcast.83) | data formatting | bytes 18874368 | tf_op jit(solution)/shard_map/while | solution.py:95
  232.7 245.5 %while.19 = (s32[]{:T(128)}, bf16[2,128,576]{1,2,0:T(8,128)(2,1)S(1)}, bf16[256,576]{0,1:T(8,128)(2,1)S(1)}, bf16[256,576]{0,1:T(8,128)(2,1)S(1)}, pred[]{:T(512...) while((s32[]{:T(128)}, ...), condition=%wide.region_5.6_spmd, body=%wide.region_0.5_spmd.sunk | while | flops 3627509248 | bytes 116467488 | solution.py:95
  232.7 0.0 all-reduce.5.cloned.1.call-start
  232.9 11.7 %all_gather.18 = bf16[128,2304]{0,1:T(8,128)(2,1)S(1)} all-gather(bf16[128,576]{0,1:T(8,128)(2,1)S(1)} %bitcast_select_fusion.4), channel_id=1, replica_groups=mesh['layer'=2,'feat'=4,'tok'=32] {'feat'}, dimensions={1}, use_global_device_ids=true | all-gather | bytes 737280 | tf_op jit(solution)/shard_map/while/body/eval_jaxpr/all_gather | solution.py:72
  244.6 0.1 conditional.2
  244.6 0.1 broadcast.16
  244.7 2.7 copy.33
  247.4 0.0 all-reduce.5.cloned.1.call-update
  247.4 0.6 dynamic-slice.29
  248.7 59.4 %all-reduce.5.cloned.1.call-done = bf16[2,128,2304]{1,0,2:T(2,128)(2,1)} async-done(((bf16[2,128,2304]{1,0,2:T(2,128)(2,1)}), bf16[2,128,2304]{1,0,2:T(2,128)(2,1)}) %all-reduce.5.cloned.1.call-update) | async-done | bytes 1179664 | tf_op jit(solution)/shard_map/while
  308.0 1.2 constant_dynamic-slice_fusion.4
  309.3 0.1 fusion.31
  309.4 0.2 fusion.30
  309.6 1.3 collective-permute-start
  310.9 2.9 collective-permute-done
  313.8 10.9 %all_gather.18 = bf16[128,2304]{0,1:T(8,128)(2,1)S(1)} all-gather(bf16[128,576]{0,1:T(8,128)(2,1)S(1)} %bitcast_select_fusion.4), channel_id=1, replica_groups=mesh['layer'=2,'feat'=4,'tok'=32] {'feat'}, dimensions={1}, use_global_device_ids=true | all-gather | bytes 737280 | tf_op jit(solution)/shard_map/while/body/eval_jaxpr/all_gather | solution.py:72
  324.8 10.8 %conditional.2 = (bf16[2,128,2304]{2,1,0:T(8,128)(2,1)S(1)}) conditional(s32[]{:T(128)} %convert_element_type.137, () %tuple.76, (bf16[1,2304,2048]{2,1,0:T(8,128)(2,1)}, bf16[128,2304]{0,1:T(8,128)(2,1)S(1)}, f32[1,2048]{1,0:T(1,128)S(1)}, s32[1,2,32]{2,1,0:T(2,128)S(1)}, s32[]{:T(128)}, /*index=5*/s32[]{:T(128)}, s32[16,1]{0,1:T(1,128)S(1)}, ...), branch_computations={%region_1.1_spmd, %region_2.3_spmd} | conditional | flops 3625518592 | bytes 100099104 | solution.py:75
  324.8 0.6 constant_dynamic-slice_fusion
  325.4 0.9 compare_bitcast_fusion
  326.3 0.2 and_reduce_fusion
  326.5 0.1 broadcast_bitcast_fusion
  326.6 5.8 %fusion.11 = bf16[128,2048]{1,0:T(8,128)(2,1)S(1)} fusion(bf16[128,2304]{0,1:T(8,128)(2,1)S(1)} %get-tuple-element.503, bf16[1,2304,2048]{2,1,0:T(8,128)(2,1)} %get-tuple-element.426, f32[2048]{0:T(1024)S(1)} %broadcast_bitcast_fusion, f32[2048]{0:T(1024)S(1)} %bitcast.86), kind=kOutput, calls=%fused_computation.7 | convolution fusion | flops 1209008128 | bytes 10567680 | tf_op jit(solution)/shard_map/while/body/eval_jaxpr/cond/branch_1_fun/dot_general | solution.py:27
  332.5 1.4 convolution_bitcast_fusion
  333.9 0.1 slice-done.2
  334.0 1.4 convolution_bitcast_fusion.1
  335.4 0.1 pad_maximum_fusion
  335.6 2.7 copy.33
  338.3 0.0 all-reduce.5.cloned.1.call-update
  338.3 0.6 dynamic-slice.29
  339.5 52.4 %all-reduce.5.cloned.1.call-done = bf16[2,128,2304]{1,0,2:T(2,128)(2,1)} async-done(((bf16[2,128,2304]{1,0,2:T(2,128)(2,1)}), bf16[2,128,2304]{1,0,2:T(2,128)(2,1)}) %all-reduce.5.cloned.1.call-update) | async-done | bytes 1179664 | tf_op jit(solution)/shard_map/while
  391.9 1.2 constant_dynamic-slice_fusion.4
  393.2 0.1 fusion.31
  393.3 0.2 fusion.30
  393.5 1.3 collective-permute-start
  394.8 2.9 collective-permute-done
  397.7 10.9 %all_gather.18 = bf16[128,2304]{0,1:T(8,128)(2,1)S(1)} all-gather(bf16[128,576]{0,1:T(8,128)(2,1)S(1)} %bitcast_select_fusion.4), channel_id=1, replica_groups=mesh['layer'=2,'feat'=4,'tok'=32] {'feat'}, dimensions={1}, use_global_device_ids=true | all-gather | bytes 737280 | tf_op jit(solution)/shard_map/while/body/eval_jaxpr/all_gather | solution.py:72
  408.7 10.8 %conditional.2 = (bf16[2,128,2304]{2,1,0:T(8,128)(2,1)S(1)}) conditional(s32[]{:T(128)} %convert_element_type.137, () %tuple.76, (bf16[1,2304,2048]{2,1,0:T(8,128)(2,1)}, bf16[128,2304]{0,1:T(8,128)(2,1)S(1)}, f32[1,2048]{1,0:T(1,128)S(1)}, s32[1,2,32]{2,1,0:T(2,128)S(1)}, s32[]{:T(128)}, /*index=5*/s32[]{:T(128)}, s32[16,1]{0,1:T(1,128)S(1)}, ...), branch_computations={%region_1.1_spmd, %region_2.3_spmd} | conditional | flops 3625518592 | bytes 100099104 | solution.py:75
  408.7 0.6 constant_dynamic-slice_fusion
  409.3 0.9 compare_bitcast_fusion
  410.2 0.2 and_reduce_fusion
  410.4 0.1 broadcast_bitcast_fusion
  410.5 5.8 %fusion.11 = bf16[128,2048]{1,0:T(8,128)(2,1)S(1)} fusion(bf16[128,2304]{0,1:T(8,128)(2,1)S(1)} %get-tuple-element.503, bf16[1,2304,2048]{2,1,0:T(8,128)(2,1)} %get-tuple-element.426, f32[2048]{0:T(1024)S(1)} %broadcast_bitcast_fusion, f32[2048]{0:T(1024)S(1)} %bitcast.86), kind=kOutput, calls=%fused_computation.7 | convolution fusion | flops 1209008128 | bytes 10567680 | tf_op jit(solution)/shard_map/while/body/eval_jaxpr/cond/branch_1_fun/dot_general | solution.py:27
  416.4 1.4 convolution_bitcast_fusion
  417.8 0.1 slice-done.2
  417.9 1.4 convolution_bitcast_fusion.1
  419.3 0.1 pad_maximum_fusion
  419.5 2.7 copy.33
  422.2 0.0 all-reduce.5.cloned.1.call-update
  422.2 0.6 dynamic-slice.29
  423.4 49.1 %all-reduce.5.cloned.1.call-done = bf16[2,128,2304]{1,0,2:T(2,128)(2,1)} async-done(((bf16[2,128,2304]{1,0,2:T(2,128)(2,1)}), bf16[2,128,2304]{1,0,2:T(2,128)(2,1)}) %all-reduce.5.cloned.1.call-update) | async-done | bytes 1179664 | tf_op jit(solution)/shard_map/while
  472.5 1.2 constant_dynamic-slice_fusion.4
  473.7 0.1 fusion.31
  473.8 0.2 fusion.30
  474.0 1.3 collective-permute-start
  475.3 2.9 collective-permute-done
  478.3 0.7 copy-done.2
  479.0 0.1 copy-done.3
  (58 shorter events, 0.6 us)
Async XLA Ops:
  7.2 109.7 %all-gather.5.cloned.1.call-start = ((), (), s32[]{:S(2)}) async-start(), calls=%async_computation | async-start | bytes 9732096 | tf_op jit(solution)/shard_map/all_gather | solution.py:53
  7.9 211.8 %all-gather.7.cloned.1.call-start = ((), (), s32[]{:S(2)}) async-start(), calls=%async_computation.1 | async-start | bytes 9732096 | tf_op jit(solution)/shard_map/all_gather | solution.py:54
  219.7 12.9 %copy-start.1 = (bf16[256,576]{0,1:T(8,128)(2,1)S(1)}, bf16[256,576]{0,1:T(8,128)(2,1)}, u32[]{:S(2)}) copy-start(bf16[256,576]{0,1:T(8,128)(2,1)} %param.15) | copy-start | bytes 884740
  219.7 13.0 %copy-start.4 = (bf16[1,256,576]{1,2,0:T(8,128)(2,1)S(1)}, bf16[1,256,576]{1,2,0:T(8,128)(2,1)}, u32[]{:S(2)}) copy-start(bf16[1,256,576]{1,2,0:T(8,128)(2,1)} %param.14) | copy-start | bytes 884740
  219.7 13.0 %copy-start.5 = (bf16[256,576]{0,1:T(8,128)(2,1)S(1)}, bf16[256,576]{0,1:T(8,128)(2,1)}, u32[]{:S(2)}) copy-start(bf16[256,576]{0,1:T(8,128)(2,1)} %param.13) | copy-start | bytes 884740
  219.7 13.0 %copy-start.6 = (f32[1,2048]{1,0:T(1,128)S(1)}, f32[1,2048]{1,0:T(1,128)}, u32[]{:S(2)}) copy-start(f32[1,2048]{1,0:T(1,128)} %param.17) | copy-start | bytes 24580
  219.7 13.0 %copy-start.7 = (s32[1,2,32]{2,1,0:T(2,128)S(1)}, s32[1,2,32]{2,1,0:T(2,128)}, u32[]{:S(2)}) copy-start(s32[1,2,32]{2,1,0:T(2,128)} %param.20) | copy-start | bytes 772
  219.7 13.0 %copy-start.8 = (s32[1,2]{1,0:T(1,128)S(1)}, s32[1,2]{1,0:T(1,128)}, u32[]{:S(2)}) copy-start(s32[1,2]{1,0:T(1,128)} %param.21) | copy-start | bytes 28
  219.7 13.0 %copy-start.9 = (u32[256]{0:T(256)S(1)}, u32[256]{0:T(256)}, u32[]{:S(2)}) copy-start(u32[256]{0:T(256)} %constant.151) | copy-start | bytes 3076
  232.7 75.3 %all-reduce.5.cloned.1.call-start = ((), (), s32[]{:S(2)}) async-start(), calls=%async_computation.2 | async-start | bytes 2359296 | tf_op jit(solution)/shard_map/while
  309.6 4.2 collective-permute-start
  313.8 78.2 %all-reduce.5.cloned.1.call-start = ((), (), s32[]{:S(2)}) async-start(), calls=%async_computation.2 | async-start | bytes 2359296 | tf_op jit(solution)/shard_map/while
  324.8 7.7 %copy-start = (bf16[2048,2304]{1,0:T(8,128)(2,1)S(1)}, bf16[2048,2304]{1,0:T(8,128)(2,1)}, u32[]{:S(2)}) copy-start(bf16[2048,2304]{1,0:T(8,128)(2,1)} %get-tuple-element.435) | copy-start | bytes 28311556 | tf_op jit(solution)/shard_map/while/body/eval_jaxpr/cond
  326.6 7.3 %slice-start = ((s8[9437184]{0:T(1024)(128)(4,1)}), s8[4194304]{0:T(1024)(128)(4,1)S(1)}, s32[]{:S(2)}) async-start(s8[9437184]{0:T(1024)(128)(4,1)} %bitcast.80), calls=%async_computation.3 | async-start | bytes 8388608 | tf_op jit(solution)/shard_map/while/body/eval_jaxpr/cond
  326.6 7.3 %slice-start.1 = ((s8[9437184]{0:T(1024)(128)(4,1)}), s8[4194304]{0:T(1024)(128)(4,1)S(1)}, s32[]{:S(2)}) async-start(s8[9437184]{0:T(1024)(128)(4,1)} %bitcast.80), calls=%async_computation.4 | async-start | bytes 8388608 | tf_op jit(solution)/shard_map/while/body/eval_jaxpr/cond
  332.5 1.5 slice-start.2
  393.5 4.2 collective-permute-start
  397.7 74.8 %all-reduce.5.cloned.1.call-start = ((), (), s32[]{:S(2)}) async-start(), calls=%async_computation.2 | async-start | bytes 2359296 | tf_op jit(solution)/shard_map/while
  408.7 7.7 %copy-start = (bf16[2048,2304]{1,0:T(8,128)(2,1)S(1)}, bf16[2048,2304]{1,0:T(8,128)(2,1)}, u32[]{:S(2)}) copy-start(bf16[2048,2304]{1,0:T(8,128)(2,1)} %get-tuple-element.435) | copy-start | bytes 28311556 | tf_op jit(solution)/shard_map/while/body/eval_jaxpr/cond
  410.5 7.3 %slice-start = ((s8[9437184]{0:T(1024)(128)(4,1)}), s8[4194304]{0:T(1024)(128)(4,1)S(1)}, s32[]{:S(2)}) async-start(s8[9437184]{0:T(1024)(128)(4,1)} %bitcast.80), calls=%async_computation.3 | async-start | bytes 8388608 | tf_op jit(solution)/shard_map/while/body/eval_jaxpr/cond
  410.5 7.3 %slice-start.1 = ((s8[9437184]{0:T(1024)(128)(4,1)}), s8[4194304]{0:T(1024)(128)(4,1)S(1)}, s32[]{:S(2)}) async-start(s8[9437184]{0:T(1024)(128)(4,1)} %bitcast.80), calls=%async_computation.4 | async-start | bytes 8388608 | tf_op jit(solution)/shard_map/while/body/eval_jaxpr/cond
  416.4 1.5 slice-start.2
  474.0 4.2 collective-permute-start
  478.3 0.7 copy-start.2
  478.3 0.8 copy-start.3
Sparse Core Ops, SparseCore 0:
  10.5 106.2 all-gather.4
  119.4 100.2 all-gather.6
  247.5 60.4 all-reduce.4
  338.4 53.4 all-reduce.4
  422.3 50.1 all-reduce.4
where the time goes:
time: 486 us
  waiting for transfers between devices  370 us (76%)
  local copies, waits for them, and re-layouts  41.3 us (8%)
  blocking collectives  33.6 us (7%)
  matrix products  17.4 us (4%)
  between operations  13.8 us (3%)
    while x6, waiting for transfers between devices  161 us
    all_gather x1, waiting for transfers between devices, shards(): lax.all_gather(dec_own[0], 'tok', axis=1, tiled=True)  108 us
    all_gather x1, waiting for transfers between devices, shards(): lax.all_gather(dec_next[0], 'tok', axis=1, tiled=True)  90.5 us
    all_gather x3, blocking collectives, advance(): gathered = lax.all_gather(residual, 'feat', axis=1, tiled=True)  33.6 us
    while x2, local copies, waits for them, and re-layouts, shards(): lax.fori_loop(0, tile_count + layer_count - 1, advance, (nothing_yet, emp...  25.2 us
    dot_general x2, matrix products, decode_every(): jnp.dot(gathered, enc_weight[0], preferred_element_type=jnp.float32)  11.7 us
  transfers between devices with their start and end apart: 8, of which 8 were waited for; matrix products, arithmetic and copies ran while one was open for 3% of the time, Pallas kernels for 0%

commit v1 on v0

--- a/solution.py
+++ b/solution.py
@@ -5,6 +5,11 @@
 
 BLOCK = 128
 TILE = 128
+
+
+def gather_from_all(x, axis, dim):
+    copies = jnp.concatenate([x] * lax.axis_size(axis), axis=dim)
+    return lax.all_to_all(copies, axis, dim, dim, tiled=True)
 
 
 def from_behind(shard, axis, by):
@@ -50,7 +55,7 @@
     columns = resid_in.shape[1]
     blocks_dev = enc_weight.shape[2] // BLOCK
     decoders = (
-        lax.all_gather(dec_own[0], "tok", axis=1, tiled=True),
+        gather_from_all(dec_own[0], "tok", 1),
         lax.all_gather(dec_next[0], "tok", axis=1, tiled=True),
     )
     empty_rows = jnp.zeros((resid_in.shape[0], columns), jnp.bfloat16)

time: 486 us -> 573 us (1.18)
  waiting for transfers between devices: 370 us -> 439 us
  starting transfers between devices: 4 us -> 16.1 us
    all_to_all x0 -> x1, waiting for transfers between devices: none -> 258 us  [gather_from_all(): return lax.all_to_all(copies, axis, dim, dim, tiled=True)]
    all_gather x1 -> x0, waiting for transfers between devices: 108 us -> none  [shards(): lax.all_gather(dec_own[0], 'tok', axis=1, tiled=True)]
    all_gather x1, waiting for transfers between devices: 90.5 us -> 0.01 us  [shards(): lax.all_gather(dec_next[0], 'tok', axis=1, tiled=True)]
    all_to_all x0 -> x1, starting transfers between devices: none -> 12.1 us  [gather_from_all(): return lax.all_to_all(copies, axis, dim, dim, tiled=True)]
    while x6, waiting for transfers between devices: 161 us -> 172 us
    concatenate x0 -> x1, local copies, waits for them, and re-layouts: none -> 5.83 us  [gather_from_all(): copies = jnp.concatenate([x] * lax.axis_size(axis), axis=dim)]
  transfers between devices with their start and end apart: 8 -> 8, of which waited for: 8 -> 7; matrix products, arithmetic and copies ran while one was open for 3% -> 2% of each run, Pallas kernels for 0% -> 0%
where the time goes in v1:
time: 573 us; the launch traced here: 572 us
  waiting for transfers between devices  439 us (77%)
  local copies, waits for them, and re-layouts  46.7 us (8%)
  blocking collectives  32.2 us (6%)
  matrix products  17.4 us (3%)
  starting transfers between devices  16.1 us (3%)
  between operations  13.8 us (2%)
    all_to_all x1, waiting for transfers between devices, gather_from_all(): return lax.all_to_all(copies, axis, dim, dim, tiled=True)  258 us
    while x6, waiting for transfers between devices  172 us
    all_gather x3, blocking collectives, advance(): gathered = lax.all_gather(residual, 'feat', axis=1, tiled=True)  32.2 us
    while x2, local copies, waits for them, and re-layouts, shards(): lax.fori_loop(0, tile_count + layer_count - 1, advance, (nothing_yet, emp...  24.7 us
    all_to_all x1, starting transfers between devices, gather_from_all(): return lax.all_to_all(copies, axis, dim, dim, tiled=True)  12.1 us
    dot_general x2, matrix products, decode_every(): jnp.dot(gathered, enc_weight[0], preferred_element_type=jnp.float32)  11.7 us
  transfers between devices with their start and end apart: 8, of which 7 were waited for; matrix products, arithmetic and copies ran while one was open for 2% of the time, Pallas kernels for 0%

profile of v1, /device:TPU:1, one launch (start us, length us, event | category | flops | bytes accessed | tf_op | source)
XLA Modules:
  0.0 571.6 jit_solution(4153172296736090958)
XLA Ops:
  7.2 5.8 %concatenate.7 = bf16[2048,32,72]{0,2,1:T(8,128)(2,1)} broadcast(bf16[2048,72]{0,1:T(8,128)(2,1)} %bitcast.86), dimensions={0,2} | broadcast | bytes 9732096 | tf_op jit(solution)/shard_map/concatenate | solution.py:11
  13.0 12.1 %all-to-all-start = ((bf16[2048,32,72]{0,2,1:T(8,128)(2,1)}), bf16[2048,32,72]{0,2,1:T(8,128)(2,1)}, u32[]{:S(2)}, u32[]{:S(2)}) async-start(bf16[2048,32,72]{0,2,1:T(8,128)(2,1)} %concatenate.7), calls=%async_computation | async-start | bytes 18874368 | tf_op jit(solution)/shard_map/all_to_all | solution.py:12
  25.1 0.0 all-gather.3.cloned.1.call-start
  25.2 0.7 all-gather.3.cloned.1.call-update
  25.9 258.2 %all-to-all-done = bf16[2048,32,72]{0,2,1:T(8,128)(2,1)} async-done(((bf16[2048,32,72]{0,2,1:T(8,128)(2,1)}), bf16[2048,32,72]{0,2,1:T(8,128)(2,1)}, u32[]{:S(2)}, u32[]{:S(2)}) %all-to-all-start) | async-done | bytes 9437216 | tf_op jit(solution)/shard_map/all_to_all | solution.py:12
  284.1 12.2 %copy.33 = bf16[2048,2304]{1,0:T(8,128)(2,1)} copy(bf16[2048,2304]{0,1:T(8,128)(2,1)} %bitcast.16) | data formatting | bytes 18874368 | tf_op jit(solution)/shard_map/while | solution.py:100
  296.3 0.0 copy-start.9
  296.3 12.6 %copy.34 = bf16[2048,2304]{1,0:T(8,128)(2,1)} copy(bf16[2048,2304]{0,1:T(8,128)(2,1)} %bitcast.83) | data formatting | bytes 18874368 | tf_op jit(solution)/shard_map/while | solution.py:100
  309.1 255.2 %while.19 = (s32[]{:T(128)}, bf16[2,128,576]{1,2,0:T(8,128)(2,1)S(1)}, bf16[256,576]{0,1:T(8,128)(2,1)S(1)}, bf16[256,576]{0,1:T(8,128)(2,1)S(1)}, pred[]{:T(512...) while((s32[]{:T(128)}, ...), condition=%wide.region_5.6_spmd, body=%wide.region_0.5_spmd.sunk | while | flops 3627509248 | bytes 116467488 | solution.py:100
  309.1 0.0 all-reduce.5.cloned.1.call-start
  309.2 10.4 %all_gather.14 = bf16[128,2304]{0,1:T(8,128)(2,1)S(1)} all-gather(bf16[128,576]{0,1:T(8,128)(2,1)S(1)} %bitcast_select_fusion.4), channel_id=1, replica_groups=mesh['layer'=2,'feat'=4,'tok'=32] {'feat'}, dimensions={1}, use_global_device_ids=true | all-gather | bytes 737280 | tf_op jit(solution)/shard_map/while/body/eval_jaxpr/all_gather | solution.py:77
  319.6 0.1 conditional.2
  319.6 0.1 broadcast.17
  319.7 2.7 copy.40
  322.4 0.0 all-reduce.5.cloned.1.call-update
  322.4 0.7 dynamic-slice.29
  323.7 70.3 %all-reduce.5.cloned.1.call-done = bf16[2,128,2304]{1,0,2:T(2,128)(2,1)} async-done(((bf16[2,128,2304]{1,0,2:T(2,128)(2,1)}), bf16[2,128,2304]{1,0,2:T(2,128)(2,1)}) %all-reduce.5.cloned.1.call-update) | async-done | bytes 1179664 | tf_op jit(solution)/shard_map/while
  394.1 1.2 constant_dynamic-slice_fusion.4
  395.3 0.1 fusion.31
  395.4 0.2 fusion.30
  395.6 1.3 collective-permute-start
  396.9 2.9 collective-permute-done
  399.8 10.9 %all_gather.14 = bf16[128,2304]{0,1:T(8,128)(2,1)S(1)} all-gather(bf16[128,576]{0,1:T(8,128)(2,1)S(1)} %bitcast_select_fusion.4), channel_id=1, replica_groups=mesh['layer'=2,'feat'=4,'tok'=32] {'feat'}, dimensions={1}, use_global_device_ids=true | all-gather | bytes 737280 | tf_op jit(solution)/shard_map/while/body/eval_jaxpr/all_gather | solution.py:77
  410.8 10.8 %conditional.2 = (bf16[2,128,2304]{2,1,0:T(8,128)(2,1)S(1)}) conditional(s32[]{:T(128)} %convert_element_type.137, () %tuple.77, (bf16[1,2304,2048]{2,1,0:T(8,128)(2,1)}, bf16[128,2304]{0,1:T(8,128)(2,1)S(1)}, f32[1,2048]{1,0:T(1,128)S(1)}, s32[1,2,32]{2,1,0:T(2,128)S(1)}, s32[]{:T(128)}, /*index=5*/s32[]{:T(128)}, s32[16,1]{0,1:T(1,128)S(1)}, ...), branch_computations={%region_1.1_spmd, %region_2.3_spmd} | conditional | flops 3625518592 | bytes 100099104 | solution.py:80
  410.8 0.6 constant_dynamic-slice_fusion
  411.4 0.9 compare_bitcast_fusion
  412.3 0.2 and_reduce_fusion
  412.5 0.1 broadcast_bitcast_fusion
  412.6 5.8 %fusion.11 = bf16[128,2048]{1,0:T(8,128)(2,1)S(1)} fusion(bf16[128,2304]{0,1:T(8,128)(2,1)S(1)} %get-tuple-element.519, bf16[1,2304,2048]{2,1,0:T(8,128)(2,1)} %get-tuple-element.426, f32[2048]{0:T(1024)S(1)} %broadcast_bitcast_fusion, f32[2048]{0:T(1024)S(1)} %bitcast.87), kind=kOutput, calls=%fused_computation.7 | convolution fusion | flops 1209008128 | bytes 10567680 | tf_op jit(solution)/shard_map/while/body/eval_jaxpr/cond/branch_1_fun/dot_general | solution.py:32
  418.4 1.4 convolution_bitcast_fusion
  419.9 0.1 slice-done.2
  420.0 1.4 convolution_bitcast_fusion.1
  421.4 0.1 pad_maximum_fusion
  421.6 2.7 copy.40
  424.2 0.0 all-reduce.5.cloned.1.call-update
  424.3 0.7 dynamic-slice.29
  425.6 52.3 %all-reduce.5.cloned.1.call-done = bf16[2,128,2304]{1,0,2:T(2,128)(2,1)} async-done(((bf16[2,128,2304]{1,0,2:T(2,128)(2,1)}), bf16[2,128,2304]{1,0,2:T(2,128)(2,1)}) %all-reduce.5.cloned.1.call-update) | async-done | bytes 1179664 | tf_op jit(solution)/shard_map/while
  477.9 1.2 constant_dynamic-slice_fusion.4
  479.1 0.1 fusion.31
  479.3 0.2 fusion.30
  479.5 1.3 collective-permute-start
  480.8 2.9 collective-permute-done
  483.7 10.9 %all_gather.14 = bf16[128,2304]{0,1:T(8,128)(2,1)S(1)} all-gather(bf16[128,576]{0,1:T(8,128)(2,1)S(1)} %bitcast_select_fusion.4), channel_id=1, replica_groups=mesh['layer'=2,'feat'=4,'tok'=32] {'feat'}, dimensions={1}, use_global_device_ids=true | all-gather | bytes 737280 | tf_op jit(solution)/shard_map/while/body/eval_jaxpr/all_gather | solution.py:77
  494.7 10.8 %conditional.2 = (bf16[2,128,2304]{2,1,0:T(8,128)(2,1)S(1)}) conditional(s32[]{:T(128)} %convert_element_type.137, () %tuple.77, (bf16[1,2304,2048]{2,1,0:T(8,128)(2,1)}, bf16[128,2304]{0,1:T(8,128)(2,1)S(1)}, f32[1,2048]{1,0:T(1,128)S(1)}, s32[1,2,32]{2,1,0:T(2,128)S(1)}, s32[]{:T(128)}, /*index=5*/s32[]{:T(128)}, s32[16,1]{0,1:T(1,128)S(1)}, ...), branch_computations={%region_1.1_spmd, %region_2.3_spmd} | conditional | flops 3625518592 | bytes 100099104 | solution.py:80
  494.7 0.6 constant_dynamic-slice_fusion
  495.3 0.9 compare_bitcast_fusion
  496.2 0.2 and_reduce_fusion
  496.4 0.1 broadcast_bitcast_fusion
  496.5 5.8 %fusion.11 = bf16[128,2048]{1,0:T(8,128)(2,1)S(1)} fusion(bf16[128,2304]{0,1:T(8,128)(2,1)S(1)} %get-tuple-element.519, bf16[1,2304,2048]{2,1,0:T(8,128)(2,1)} %get-tuple-element.426, f32[2048]{0:T(1024)S(1)} %broadcast_bitcast_fusion, f32[2048]{0:T(1024)S(1)} %bitcast.87), kind=kOutput, calls=%fused_computation.7 | convolution fusion | flops 1209008128 | bytes 10567680 | tf_op jit(solution)/shard_map/while/body/eval_jaxpr/cond/branch_1_fun/dot_general | solution.py:32
  502.3 1.4 convolution_bitcast_fusion
  503.8 0.1 slice-done.2
  503.9 1.4 convolution_bitcast_fusion.1
  505.3 0.1 pad_maximum_fusion
  505.4 2.7 copy.40
  508.1 0.0 all-reduce.5.cloned.1.call-update
  508.2 0.7 dynamic-slice.29
  509.5 49.0 %all-reduce.5.cloned.1.call-done = bf16[2,128,2304]{1,0,2:T(2,128)(2,1)} async-done(((bf16[2,128,2304]{1,0,2:T(2,128)(2,1)}), bf16[2,128,2304]{1,0,2:T(2,128)(2,1)}) %all-reduce.5.cloned.1.call-update) | async-done | bytes 1179664 | tf_op jit(solution)/shard_map/while
  558.5 1.2 constant_dynamic-slice_fusion.4
  559.7 0.1 fusion.31
  559.8 0.2 fusion.30
  560.0 1.3 collective-permute-start
  561.3 2.9 collective-permute-done
  564.2 0.7 copy-done.2
  565.0 0.1 copy-done.3
  (58 shorter events, 0.6 us)
Async XLA Ops:
  13.0 271.1 %all-to-all-start = ((bf16[2048,32,72]{0,2,1:T(8,128)(2,1)}), bf16[2048,32,72]{0,2,1:T(8,128)(2,1)}, u32[]{:S(2)}, u32[]{:S(2)}) async-start(bf16[2048,32,72]{0,2,1:T(8,128)(2,1)} %concatenate.7), calls=%async_computation | async-start | bytes 18874368 | tf_op jit(solution)/shard_map/all_to_all | solution.py:12
  25.1 271.1 %all-gather.3.cloned.1.call-start = ((), (), s32[]{:S(2)}) async-start(), calls=%async_computation.1 | async-start | bytes 9732096 | tf_op jit(solution)/shard_map/all_gather | solution.py:59
  296.3 12.7 %copy-start.1 = (bf16[256,576]{0,1:T(8,128)(2,1)S(1)}, bf16[256,576]{0,1:T(8,128)(2,1)}, u32[]{:S(2)}) copy-start(bf16[256,576]{0,1:T(8,128)(2,1)} %param.15) | copy-start | bytes 884740
  296.3 12.7 %copy-start.4 = (bf16[1,256,576]{1,2,0:T(8,128)(2,1)S(1)}, bf16[1,256,576]{1,2,0:T(8,128)(2,1)}, u32[]{:S(2)}) copy-start(bf16[1,256,576]{1,2,0:T(8,128)(2,1)} %param.14) | copy-start | bytes 884740
  296.3 12.7 %copy-start.5 = (bf16[256,576]{0,1:T(8,128)(2,1)S(1)}, bf16[256,576]{0,1:T(8,128)(2,1)}, u32[]{:S(2)}) copy-start(bf16[256,576]{0,1:T(8,128)(2,1)} %param.13) | copy-start | bytes 884740
  296.3 12.8 %copy-start.6 = (f32[1,2048]{1,0:T(1,128)S(1)}, f32[1,2048]{1,0:T(1,128)}, u32[]{:S(2)}) copy-start(f32[1,2048]{1,0:T(1,128)} %param.17) | copy-start | bytes 24580
  296.3 12.7 %copy-start.7 = (s32[1,2,32]{2,1,0:T(2,128)S(1)}, s32[1,2,32]{2,1,0:T(2,128)}, u32[]{:S(2)}) copy-start(s32[1,2,32]{2,1,0:T(2,128)} %param.20) | copy-start | bytes 772
  296.3 12.7 %copy-start.8 = (s32[1,2]{1,0:T(1,128)S(1)}, s32[1,2]{1,0:T(1,128)}, u32[]{:S(2)}) copy-start(s32[1,2]{1,0:T(1,128)} %param.21) | copy-start | bytes 28
  296.3 12.7 %copy-start.9 = (u32[256]{0:T(256)S(1)}, u32[256]{0:T(256)}, u32[]{:S(2)}) copy-start(u32[256]{0:T(256)} %constant.151) | copy-start | bytes 3076
  309.1 85.0 %all-reduce.5.cloned.1.call-start = ((), (), s32[]{:S(2)}) async-start(), calls=%async_computation.2 | async-start | bytes 2359296 | tf_op jit(solution)/shard_map/while
  395.6 4.2 collective-permute-start
  399.8 78.1 %all-reduce.5.cloned.1.call-start = ((), (), s32[]{:S(2)}) async-start(), calls=%async_computation.2 | async-start | bytes 2359296 | tf_op jit(solution)/shard_map/while
  410.8 7.6 %copy-start = (bf16[2048,2304]{1,0:T(8,128)(2,1)S(1)}, bf16[2048,2304]{1,0:T(8,128)(2,1)}, u32[]{:S(2)}) copy-start(bf16[2048,2304]{1,0:T(8,128)(2,1)} %get-tuple-element.435) | copy-start | bytes 28311556 | tf_op jit(solution)/shard_map/while/body/eval_jaxpr/cond
  412.6 7.3 %slice-start = ((s8[9437184]{0:T(1024)(128)(4,1)}), s8[4194304]{0:T(1024)(128)(4,1)S(1)}, s32[]{:S(2)}) async-start(s8[9437184]{0:T(1024)(128)(4,1)} %bitcast.81), calls=%async_computation.3 | async-start | bytes 8388608 | tf_op jit(solution)/shard_map/while/body/eval_jaxpr/cond
  412.6 7.3 %slice-start.1 = ((s8[9437184]{0:T(1024)(128)(4,1)}), s8[4194304]{0:T(1024)(128)(4,1)S(1)}, s32[]{:S(2)}) async-start(s8[9437184]{0:T(1024)(128)(4,1)} %bitcast.81), calls=%async_computation.4 | async-start | bytes 8388608 | tf_op jit(solution)/shard_map/while/body/eval_jaxpr/cond
  418.4 1.6 slice-start.2
  479.5 4.2 collective-permute-start
  483.7 74.8 %all-reduce.5.cloned.1.call-start = ((), (), s32[]{:S(2)}) async-start(), calls=%async_computation.2 | async-start | bytes 2359296 | tf_op jit(solution)/shard_map/while
  494.7 7.6 %copy-start = (bf16[2048,2304]{1,0:T(8,128)(2,1)S(1)}, bf16[2048,2304]{1,0:T(8,128)(2,1)}, u32[]{:S(2)}) copy-start(bf16[2048,2304]{1,0:T(8,128)(2,1)} %get-tuple-element.435) | copy-start | bytes 28311556 | tf_op jit(solution)/shard_map/while/body/eval_jaxpr/cond
  496.5 7.3 %slice-start = ((s8[9437184]{0:T(1024)(128)(4,1)}), s8[4194304]{0:T(1024)(128)(4,1)S(1)}, s32[]{:S(2)}) async-start(s8[9437184]{0:T(1024)(128)(4,1)} %bitcast.81), calls=%async_computation.3 | async-start | bytes 8388608 | tf_op jit(solution)/shard_map/while/body/eval_jaxpr/cond
  496.5 7.3 %slice-start.1 = ((s8[9437184]{0:T(1024)(128)(4,1)}), s8[4194304]{0:T(1024)(128)(4,1)S(1)}, s32[]{:S(2)}) async-start(s8[9437184]{0:T(1024)(128)(4,1)} %bitcast.81), calls=%async_computation.4 | async-start | bytes 8388608 | tf_op jit(solution)/shard_map/while/body/eval_jaxpr/cond
  502.3 1.6 slice-start.2
  560.0 4.2 collective-permute-start
  564.2 0.7 copy-start.2
  564.2 0.8 copy-start.3
Sparse Core Ops, SparseCore 0:
  28.5 243.1 all-gather.2
  322.5 71.5 all-reduce.4
  424.4 53.4 all-reduce.4
  508.3 50.1 all-reduce.4
